TPU v7x, 32 devices: a whole 2x2x4 slice. The times are simulated.
32 devices in a mesh: sec: 4 (over y, x), tile: 8 (over z, core).
Axes of the slice: x: 2, y: 2, z: 4, core: 2. Of those that a mesh axis runs over, the one named last changes fastest.
Arguments:
- tracers: bfloat16 [4, 72, 32, 1024], P(None, None, 'sec', 'tile'), may hold values from -6 to 6
- courant: bfloat16 [2, 72, 32, 1024], P(None, None, 'sec', 'tile'), may hold values from -0.44921875 to 0.44921875
- destination: int32 [32, 8], P(('sec', 'tile')), may hold values from 0 to 7, each once within a row
- diffusion: bfloat16 [32, 72, 72], P(('sec', 'tile')), may hold values from 0 to 1.25
- band: int32 [32], P(('sec', 'tile')), may hold values from 0 to 15
- band_table: bfloat16 [16, 72, 72], replicated, may hold values from -0.75 to 0.75
Outputs:
- column_state: bfloat16 [4, 72, 256, 128], P(None, None, ('sec', 'tile'))
Inputs may be any that keep to these rules, and one draw needn't show every extreme that they name: Each row of destination names every column block of its group once.
All inputs are finite; a program needn't handle non-finite values.
Results may differ from a plain program's by a relative error of at most 0.0066.
Values may be sent and summed in bfloat16 or wider, within the bound.
No kernel may reach another device: no remote copies, remote signals or barrier semaphores. Data moves between devices by JAX's collectives and lax.ppermute only.
A program may use at most 128 MiB of HBM per device.

v0:
```python
import jax
import jax.numpy as jnp
from jax import lax
from jax.sharding import PartitionSpec as P

STEPS = 3


def with_halo(cells, sides, width):
    for axis, dim in sides:
        count = lax.axis_size(axis)
        head = lax.slice_in_dim(cells, 0, width, axis=dim)
        tail = lax.slice_in_dim(cells, cells.shape[dim] - width, cells.shape[dim], axis=dim)
        cells = jnp.concatenate(
            [
                lax.ppermute(tail, axis, [(i, (i + 1) % count) for i in range(count)]),
                cells,
                lax.ppermute(head, axis, [((i + 1) % count, i) for i in range(count)]),
            ],
            axis=dim,
        )
    return cells


def advect_tile(padded, courant):
    centre = padded[:, :, 1:-1, 1:-1].astype(jnp.float32)
    north = padded[:, :, 2:, 1:-1].astype(jnp.float32)
    south = padded[:, :, :-2, 1:-1].astype(jnp.float32)
    east = padded[:, :, 1:-1, 2:].astype(jnp.float32)
    west = padded[:, :, 1:-1, :-2].astype(jnp.float32)
    cx = courant[0].astype(jnp.float32)
    cy = courant[1].astype(jnp.float32)
    out = centre - 0.5 * cx * (north - south) + 0.5 * cx * cx * (north - 2.0 * centre + south)
    out = out - 0.5 * cy * (east - west) + 0.5 * cy * cy * (east - 2.0 * centre + west)
    return out.astype(jnp.bfloat16)


def substep(field, courant):
    padded = with_halo(field, (("sec", 2), ("tile", 3)), 1)
    return advect_tile(padded, courant)


def per_device(tracers, courant, destination, diffusion, band, band_table):
    advected = tracers
    for step in range(STEPS):
        advected = substep(advected, courant)
    order = jnp.argsort(destination[0])
    band_count = band_table.shape[0]
    ordered = jnp.take(advected, order, axis=2)
    received = lax.all_to_all(ordered, "tile", split_axis=2, concat_axis=2, tiled=True)
    inverse = diffusion[0]
    diffused = jnp.einsum("kl,tlxy->tkxy", inverse, received, preferred_element_type=jnp.float32)
    diffused16 = diffused.astype(jnp.bfloat16)
    picked = (jnp.arange(band_count, dtype=jnp.int32) == band[0])[:, None, None]
    radiation = jnp.sum(jnp.where(picked, band_table, jnp.zeros_like(band_table)), axis=0)
    heating = jnp.einsum("kl,tlxy->tkxy", radiation, diffused16, preferred_element_type=jnp.float32)
    return (diffused + heating).astype(jnp.bfloat16)


def solution(mesh):
    placed = (
        P(None, None, "sec", "tile"),
        P(None, None, "sec", "tile"),
        P(("sec", "tile"), None),
        P(("sec", "tile"), None, None),
        P(("sec", "tile")),
        P(),
    )
    return jax.shard_map(
        per_device,
        mesh=mesh,
        in_specs=placed,
        out_specs=P(None, None, ("sec", "tile"), None),
        check_vma=False,
    )
```

profile of v0, /device:TPU:0, one launch (start us, length us, event | category | flops | bytes accessed | tf_op | source)
XLA Modules:
  0.0 81.5 jit_solution(5658749465886377989)
XLA Ops:
  0.0 1.2 %copy.20 = bf16[4,72,8,128]{3,1,2,0:T(8,128)(2,1)S(1)} copy(bf16[4,72,8,128]{3,2,1,0:T(8,128)(2,1)} %param.6) | data formatting | bytes 1179648 | tf_op args[0]
  1.2 3.0 %collective-permute-start.1 = (bf16[4,72,1,128]{3,1,2,0:T(8,128)(2,1)S(1)}, bf16[4,72,1,128]{3,1,2,0:T(8,128)(2,1)S(1)}, u32[]{:S(2)}, u32[]{:S(2)}) collective-permute-start(bf16[4,72,1,128]{3,1,2,0:T(8,128)(2,1)S(1)} %get-tuple-element.18), channel_id=1, source_target_pairs={{0,8},{8,16},{16,24},{24,0},{1,9},{9,17},{17,25},{25,1},{2,10},{10... | collective-permute-start | bytes 221192 | tf_op jit(solution)/shard_map/ppermute | solution.py:16
  4.2 1.0 %collective-permute-start = (bf16[4,72,1,128]{3,1,2,0:T(8,128)(2,1)S(1)}, bf16[4,72,1,128]{3,1,2,0:T(8,128)(2,1)S(1)}, u32[]{:S(2)}, u32[]{:S(2)}) collective-permute-start(bf16[4,72,1,128]{3,1,2,0:T(8,128)(2,1)S(1)} %get-tuple-element.17), channel_id=1, source_target_pairs={{8,0},{16,8},{24,16},{0,24},{9,1},{17,9},{25,17},{1,25},{10,2},{18... | collective-permute-start | bytes 221192 | tf_op jit(solution)/shard_map/ppermute | solution.py:18
  5.3 2.5 %collective-permute-done.1 = bf16[4,72,1,128]{3,1,2,0:T(8,128)(2,1)S(1)} collective-permute-done((bf16[4,72,1,128]{3,1,2,0:T(8,128)(2,1)S(1)}, bf16[4,72,1,128]{3,1,2,0:T(8,128)(2,1)S(1)}, u32[]{:S(2)}, u32[]{:S(2)}) %collective-permute-start.1) | collective-permute-done | bytes 73760 | tf_op jit(solution)/shard_map/ppermute | solution.py:16
  7.9 1.4 %collective-permute-done = bf16[4,72,1,128]{3,1,2,0:T(8,128)(2,1)S(1)} collective-permute-done((bf16[4,72,1,128]{3,1,2,0:T(8,128)(2,1)S(1)}, bf16[4,72,1,128]{3,1,2,0:T(8,128)(2,1)S(1)}, u32[]{:S(2)}, u32[]{:S(2)}) %collective-permute-start) | collective-permute-done | bytes 73760 | tf_op jit(solution)/shard_map/ppermute | solution.py:18
  9.3 1.1 %fusion.36 = (bf16[4,72,10,1]{3,1,2,0:T(8,128)(2,1)}, bf16[4,72,10,1]{3,1,2,0:T(8,128)(2,1)S(1)}) fusion(bf16[4,72,10,128]{3,1,2,0:T(8,128)(2,1)S(1)} %constant_dynamic-update-slice_fusion), kind=kLoop, calls=%fused_computation.97 | loop fusion | bytes 23040 | tf_op jit(solution)/shard_map/slice | solution.py:12
  10.4 1.5 %copy.29 = bf16[4,72,10,1]{1,0,3,2:T(4,128)(2,1)S(1)} copy(bf16[4,72,10,1]{3,1,2,0:T(8,128)(2,1)} %get-tuple-element.11) | data formatting | bytes 11520 | tf_op jit(solution)/shard_map/slice | solution.py:12
  11.9 2.2 %collective-permute-start.2 = (bf16[4,72,10,1]{1,0,3,2:T(4,128)(2,1)S(1)}, bf16[4,72,10,1]{1,0,3,2:T(4,128)(2,1)S(1)}, u32[]{:S(2)}, u32[]{:S(2)}) collective-permute-start(bf16[4,72,10,1]{1,0,3,2:T(4,128)(2,1)S(1)} %copy.29), channel_id=1, source_target_pairs={{1,0},{2,1},{3,2},{4,3},{5,4},{6,5},{7,6},{0,7},{9,8},{10,9},{11,1... | collective-permute-start | bytes 17288 | tf_op jit(solution)/shard_map/ppermute | solution.py:18
  15.5 1.2 %copy.30 = bf16[4,72,10,1]{3,1,2,0:T(8,128)(2,1)} copy(bf16[4,72,10,1]{1,0,3,2:T(4,128)(2,1)S(1)} %collective-permute-done.2) | data formatting | bytes 11520 | tf_op jit(solution)/shard_map/ppermute | solution.py:18
  16.8 2.6 %collective-permute-done.3 = bf16[4,72,10,1]{1,0,3,2:T(4,128)(2,1)S(1)} collective-permute-done((bf16[4,72,10,1]{1,0,3,2:T(4,128)(2,1)S(1)}, bf16[4,72,10,1]{1,0,3,2:T(4,128)(2,1)S(1)}, u32[]{:S(2)}, u32[]{:S(2)}) %collective-permute-start.3) | collective-permute-done | bytes 5792 | tf_op jit(solution)/shard_map/ppermute | solution.py:16
  19.4 1.2 %copy.32 = bf16[4,72,10,1]{3,1,2,0:T(8,128)(2,1)} copy(bf16[4,72,10,1]{1,0,3,2:T(4,128)(2,1)S(1)} %collective-permute-done.3) | data formatting | bytes 11520 | tf_op jit(solution)/shard_map/ppermute | solution.py:16
  20.6 2.5 %fusion.5 = bf16[4,72,8,128]{3,1,2,0:T(8,128)(2,1)S(1)} fusion(bf16[4,72,8,128]{3,1,2,0:T(8,128)(2,1)S(1)} %copy.20, bf16[4,72,10,128]{3,1,2,0:T(8,128)(2,1)S(1)} %constant_dynamic-update-slice_fusion, bf16[4,72,10,1]{3,1,2,0:T(8,128)(2,1)} %copy.32, bf16[4,72,10,1]{3,1,2,0:T(8,128)(2,1)} %copy.30, bf16[4,72,1,128]{3,1,2,0:T(8,128)(2,1)S(1)} %collective-permute-done.1, ...), kind=kLoop, calls=%fused_computation.31 | loop fusion | flops 9732096 | bytes 3255552 | tf_op jit(solution)/shard_map/convert_element_type | solution.py:35
  23.1 2.2 %collective-permute-start.4 = (bf16[4,72,1,128]{3,1,2,0:T(8,128)(2,1)S(1)}, bf16[4,72,1,128]{3,1,2,0:T(8,128)(2,1)S(1)}, u32[]{:S(2)}, u32[]{:S(2)}) collective-permute-start(bf16[4,72,1,128]{3,1,2,0:T(8,128)(2,1)S(1)} %get-tuple-element.16), channel_id=1, source_target_pairs={{8,0},{16,8},{24,16},{0,24},{9,1},{17,9},{25,17},{1,25},{10,2},{18... | collective-permute-start | bytes 221192 | tf_op jit(solution)/shard_map/ppermute | solution.py:18
  25.5 1.0 %sort.17 = (s32[8]{0:T(128)}, s32[8]{0:T(128)S(1)}) sort(s32[8]{0:T(128)S(1)} %bitcast.30, s32[8]{0:T(128)S(1)} %iota.9), dimensions={0}, to_apply=%region_0.0 | sort | flops 24 | bytes 128 | tf_op jit(solution)/shard_map/jit(argsort)/sort | solution.py:47
  26.4 1.3 %collective-permute-done.4 = bf16[4,72,1,128]{3,1,2,0:T(8,128)(2,1)S(1)} collective-permute-done((bf16[4,72,1,128]{3,1,2,0:T(8,128)(2,1)S(1)}, bf16[4,72,1,128]{3,1,2,0:T(8,128)(2,1)S(1)}, u32[]{:S(2)}, u32[]{:S(2)}) %collective-permute-start.4) | collective-permute-done | bytes 73760 | tf_op jit(solution)/shard_map/ppermute | solution.py:18
  27.7 2.9 %collective-permute-done.5 = bf16[4,72,1,128]{3,1,2,0:T(8,128)(2,1)S(1)} collective-permute-done((bf16[4,72,1,128]{3,1,2,0:T(8,128)(2,1)S(1)}, bf16[4,72,1,128]{3,1,2,0:T(8,128)(2,1)S(1)}, u32[]{:S(2)}, u32[]{:S(2)}) %collective-permute-start.5) | collective-permute-done | bytes 73760 | tf_op jit(solution)/shard_map/ppermute | solution.py:16
  30.7 1.1 %fusion.35 = (bf16[4,72,10,1]{3,1,2,0:T(8,128)(2,1)}, bf16[4,72,10,1]{3,1,2,0:T(8,128)(2,1)S(1)}) fusion(bf16[4,72,10,128]{3,1,2,0:T(8,128)(2,1)S(1)} %pad_maximum_fusion), kind=kLoop, calls=%fused_computation.96 | loop fusion | bytes 23040 | tf_op jit(solution)/shard_map/slice | solution.py:12
  31.8 1.4 %copy.34 = bf16[4,72,10,1]{1,0,3,2:T(4,128)(2,1)S(1)} copy(bf16[4,72,10,1]{3,1,2,0:T(8,128)(2,1)} %get-tuple-element.9) | data formatting | bytes 11520 | tf_op jit(solution)/shard_map/slice | solution.py:12
  35.2 3.5 %collective-permute-done.7 = bf16[4,72,10,1]{1,0,3,2:T(4,128)(2,1)S(1)} collective-permute-done((bf16[4,72,10,1]{1,0,3,2:T(4,128)(2,1)S(1)}, bf16[4,72,10,1]{1,0,3,2:T(4,128)(2,1)S(1)}, u32[]{:S(2)}, u32[]{:S(2)}) %collective-permute-start.7) | collective-permute-done | bytes 5792 | tf_op jit(solution)/shard_map/ppermute | solution.py:16
  38.6 1.2 %copy.37 = bf16[4,72,10,1]{3,1,2,0:T(8,128)(2,1)} copy(bf16[4,72,10,1]{1,0,3,2:T(4,128)(2,1)S(1)} %collective-permute-done.7) | data formatting | bytes 11520 | tf_op jit(solution)/shard_map/ppermute | solution.py:16
  39.8 2.3 %fusion.13 = bf16[4,72,8,128]{3,1,2,0:T(8,128)(2,1)S(1)} fusion(bf16[4,72,8,128]{3,1,2,0:T(8,128)(2,1)S(1)} %fusion.5, bf16[4,72,10,1]{3,1,2,0:T(8,128)(2,1)} %copy.37, bf16[4,72,1,128]{3,1,2,0:T(8,128)(2,1)S(1)} %collective-permute-done.4, bf16[4,72,1,128]{3,1,2,0:T(8,128)(2,1)S(1)} %collective-permute-done.5, bf16[4,72,10,1]{3,1,2,0:T(8,128)(2,1)S(1)} %copy.35, ...), kind=kLoop, calls=%fused_computation.39 | loop fusion | flops 12091392 | bytes 2518272 | tf_op jit(solution)/shard_map/convert_element_type | solution.py:35
  42.2 1.2 %collective-permute-start.8 = (bf16[4,72,1,128]{3,1,2,0:T(8,128)(2,1)S(1)}, bf16[4,72,1,128]{3,1,2,0:T(8,128)(2,1)S(1)}, u32[]{:S(2)}, u32[]{:S(2)}) collective-permute-start(bf16[4,72,1,128]{3,1,2,0:T(8,128)(2,1)S(1)} %get-tuple-element.14), channel_id=1, source_target_pairs={{8,0},{16,8},{24,16},{0,24},{9,1},{17,9},{25,17},{1,25},{10,2},{18... | collective-permute-start | bytes 221192 | tf_op jit(solution)/shard_map/ppermute | solution.py:18
  43.3 0.9 %collective-permute-start.9 = (bf16[4,72,1,128]{3,1,2,0:T(8,128)(2,1)S(1)}, bf16[4,72,1,128]{3,1,2,0:T(8,128)(2,1)S(1)}, u32[]{:S(2)}, u32[]{:S(2)}) collective-permute-start(bf16[4,72,1,128]{3,1,2,0:T(8,128)(2,1)S(1)} %get-tuple-element.13), channel_id=1, source_target_pairs={{0,8},{8,16},{16,24},{24,0},{1,9},{9,17},{17,25},{25,1},{2,10},{10... | collective-permute-start | bytes 221192 | tf_op jit(solution)/shard_map/ppermute | solution.py:16
  44.2 2.3 %collective-permute-done.8 = bf16[4,72,1,128]{3,1,2,0:T(8,128)(2,1)S(1)} collective-permute-done((bf16[4,72,1,128]{3,1,2,0:T(8,128)(2,1)S(1)}, bf16[4,72,1,128]{3,1,2,0:T(8,128)(2,1)S(1)}, u32[]{:S(2)}, u32[]{:S(2)}) %collective-permute-start.8) | collective-permute-done | bytes 73760 | tf_op jit(solution)/shard_map/ppermute | solution.py:18
  46.6 2.0 %collective-permute-done.9 = bf16[4,72,1,128]{3,1,2,0:T(8,128)(2,1)S(1)} collective-permute-done((bf16[4,72,1,128]{3,1,2,0:T(8,128)(2,1)S(1)}, bf16[4,72,1,128]{3,1,2,0:T(8,128)(2,1)S(1)}, u32[]{:S(2)}, u32[]{:S(2)}) %collective-permute-start.9) | collective-permute-done | bytes 73760 | tf_op jit(solution)/shard_map/ppermute | solution.py:16
  51.2 3.5 %collective-permute-done.11 = bf16[4,72,10,1]{1,0,3,2:T(4,128)(2,1)S(1)} collective-permute-done((bf16[4,72,10,1]{1,0,3,2:T(4,128)(2,1)S(1)}, bf16[4,72,10,1]{1,0,3,2:T(4,128)(2,1)S(1)}, u32[]{:S(2)}, u32[]{:S(2)}) %collective-permute-start.11) | collective-permute-done | bytes 5792 | tf_op jit(solution)/shard_map/ppermute | solution.py:16
  55.1 2.0 %fusion.21 = bf16[4,72,8,128]{3,1,2,0:T(8,128)(2,1)} fusion(bf16[4,72,8,128]{3,1,2,0:T(8,128)(2,1)S(1)} %fusion.13, bf16[4,72,10,1]{3,1,2,0:T(8,128)(2,1)S(1)} %copy.41, bf16[4,72,1,128]{3,1,2,0:T(8,128)(2,1)S(1)} %collective-permute-done.8, bf16[4,72,1,128]{3,1,2,0:T(8,128)(2,1)S(1)} %collective-permute-done.9, bf16[4,72,10,1]{3,1,2,0:T(8,128)(2,1)S(1)} %copy.39, ...), kind=kLoop, calls=%fused_computation.47 | loop fusion | flops 12091392 | bytes 2518272 | tf_op jit(solution)/shard_map/convert_element_type | solution.py:35
  57.1 1.7 %gather_fusion = bf16[8,4,72,128]{3,2,1,0:T(8,128)(2,1)S(1)} fusion(bf16[4,72,8,128]{3,1,2,0:T(8,128)(2,1)} %fusion.21, s32[1024]{0:T(1024)S(1)} %pad_clamp_fusion), kind=kCustom, calls=%fused_computation | custom fusion | bytes 1179680 | tf_op jit(solution)/shard_map/jit(_take)/gather | solution.py:49
  58.9 0.9 %select_bitcast_fusion = bf16[4,72,8,128]{3,1,0,2:T(8,128)(2,1)} fusion(bf16[8,4,72,128]{3,2,1,0:T(8,128)(2,1)S(1)} %gather_fusion, pred[8]{0:T(512)(128)(4,1)S(1)} %compare_and_fusion), kind=kLoop, calls=%fused_computation.77 | loop fusion | flops 294912 | bytes 1179656 | tf_op jit(solution)/shard_map/jit(_take)/select_n | solution.py:49
  59.8 3.5 %all-to-all-start = ((bf16[4,72,8,128]{3,1,0,2:T(8,128)(2,1)}), bf16[4,72,8,128]{3,1,0,2:T(8,128)(2,1)S(1)}, u32[]{:S(2)}, u32[]{:S(2)}) async-start(bf16[4,72,8,128]{3,1,0,2:T(8,128)(2,1)} %select_bitcast_fusion), calls=%async_computation | async-start | bytes 1179648 | tf_op jit(solution)/shard_map/all_to_all | solution.py:50
  64.2 15.9 %all-to-all-done = bf16[4,72,8,128]{3,1,0,2:T(8,128)(2,1)S(1)} async-done(((bf16[4,72,8,128]{3,1,0,2:T(8,128)(2,1)}), bf16[4,72,8,128]{3,1,0,2:T(8,128)(2,1)S(1)}, u32[]{:S(2)}, u32[]{:S(2)}) %all-to-all-start) | async-done | bytes 589856 | tf_op jit(solution)/shard_map/all_to_all | solution.py:50
  80.6 0.9 %copy.43 = bf16[4,72,8,128]{3,2,1,0:T(8,128)(2,1)} copy(bf16[4,72,8,128]{3,1,2,0:T(8,128)(2,1)S(1)} %fusion.1) | data formatting | bytes 1179648 | tf_op jit(solution)/shard_map/convert_element_type | solution.py:57
  (48 shorter events, 7.4 us)
Async XLA Ops:
  0.0 80.0 %copy-start = (bf16[1,72,72]{2,1,0:T(8,128)(2,1)S(1)}, bf16[1,72,72]{2,1,0:T(8,128)(2,1)}, u32[]{:S(2)}) copy-start(bf16[1,72,72]{2,1,0:T(8,128)(2,1)} %param.9) | copy-start | bytes 31108
  0.0 7.8 %copy-start.1 = (bf16[4,72,8,128]{3,2,1,0:T(8,128)(2,1)S(1)}, bf16[4,72,8,128]{3,2,1,0:T(8,128)(2,1)}, u32[]{:S(2)}) copy-start(bf16[4,72,8,128]{3,2,1,0:T(8,128)(2,1)} %param.6) | copy-start | bytes 1769476
  1.2 6.5 %collective-permute-start.1 = (bf16[4,72,1,128]{3,1,2,0:T(8,128)(2,1)S(1)}, bf16[4,72,1,128]{3,1,2,0:T(8,128)(2,1)S(1)}, u32[]{:S(2)}, u32[]{:S(2)}) collective-permute-start(bf16[4,72,1,128]{3,1,2,0:T(8,128)(2,1)S(1)} %get-tuple-element.18), channel_id=1, source_target_pairs={{0,8},{8,16},{16,24},{24,0},{1,9},{9,17},{17,25},{25,1},{2,10},{10... | collective-permute-start | bytes 221192 | tf_op jit(solution)/shard_map/ppermute | solution.py:16
  4.2 5.1 %collective-permute-start = (bf16[4,72,1,128]{3,1,2,0:T(8,128)(2,1)S(1)}, bf16[4,72,1,128]{3,1,2,0:T(8,128)(2,1)S(1)}, u32[]{:S(2)}, u32[]{:S(2)}) collective-permute-start(bf16[4,72,1,128]{3,1,2,0:T(8,128)(2,1)S(1)} %get-tuple-element.17), channel_id=1, source_target_pairs={{8,0},{16,8},{24,16},{0,24},{9,1},{17,9},{25,17},{1,25},{10,2},{18... | collective-permute-start | bytes 221192 | tf_op jit(solution)/shard_map/ppermute | solution.py:18
  10.4 4.1 %copy-start.3 = (bf16[2,72,8,128]{3,2,1,0:T(8,128)(2,1)S(1)}, bf16[2,72,8,128]{3,2,1,0:T(8,128)(2,1)}, u32[]{:S(2)}) copy-start(bf16[2,72,8,128]{3,2,1,0:T(8,128)(2,1)} %param.7) | copy-start | bytes 884740
  11.9 3.6 %collective-permute-start.2 = (bf16[4,72,10,1]{1,0,3,2:T(4,128)(2,1)S(1)}, bf16[4,72,10,1]{1,0,3,2:T(4,128)(2,1)S(1)}, u32[]{:S(2)}, u32[]{:S(2)}) collective-permute-start(bf16[4,72,10,1]{1,0,3,2:T(4,128)(2,1)S(1)} %copy.29), channel_id=1, source_target_pairs={{1,0},{2,1},{3,2},{4,3},{5,4},{6,5},{7,6},{0,7},{9,8},{10,9},{11,1... | collective-permute-start | bytes 17288 | tf_op jit(solution)/shard_map/ppermute | solution.py:18
  14.5 4.9 %collective-permute-start.3 = (bf16[4,72,10,1]{1,0,3,2:T(4,128)(2,1)S(1)}, bf16[4,72,10,1]{1,0,3,2:T(4,128)(2,1)S(1)}, u32[]{:S(2)}, u32[]{:S(2)}) collective-permute-start(bf16[4,72,10,1]{1,0,3,2:T(4,128)(2,1)S(1)} %copy.31), channel_id=1, source_target_pairs={{0,1},{1,2},{2,3},{3,4},{4,5},{5,6},{6,7},{7,0},{8,9},{9,10},{10,1... | collective-permute-start | bytes 17288 | tf_op jit(solution)/shard_map/ppermute | solution.py:16
  20.6 4.8 %copy-start.4 = (s32[1,8]{1,0:T(1,128)S(1)}, s32[1,8]{1,0:T(1,128)}, u32[]{:S(2)}) copy-start(s32[1,8]{1,0:T(1,128)} %param.8) | copy-start | bytes 100
  23.1 4.6 %collective-permute-start.4 = (bf16[4,72,1,128]{3,1,2,0:T(8,128)(2,1)S(1)}, bf16[4,72,1,128]{3,1,2,0:T(8,128)(2,1)S(1)}, u32[]{:S(2)}, u32[]{:S(2)}) collective-permute-start(bf16[4,72,1,128]{3,1,2,0:T(8,128)(2,1)S(1)} %get-tuple-element.16), channel_id=1, source_target_pairs={{8,0},{16,8},{24,16},{0,24},{9,1},{17,9},{25,17},{1,25},{10,2},{18... | collective-permute-start | bytes 221192 | tf_op jit(solution)/shard_map/ppermute | solution.py:18
  25.4 5.3 %collective-permute-start.5 = (bf16[4,72,1,128]{3,1,2,0:T(8,128)(2,1)S(1)}, bf16[4,72,1,128]{3,1,2,0:T(8,128)(2,1)S(1)}, u32[]{:S(2)}, u32[]{:S(2)}) collective-permute-start(bf16[4,72,1,128]{3,1,2,0:T(8,128)(2,1)S(1)} %get-tuple-element.15), channel_id=1, source_target_pairs={{0,8},{8,16},{16,24},{24,0},{1,9},{9,17},{17,25},{25,1},{2,10},{10... | collective-permute-start | bytes 221192 | tf_op jit(solution)/shard_map/ppermute | solution.py:16
  33.3 1.4 %collective-permute-start.6 = (bf16[4,72,10,1]{1,0,3,2:T(4,128)(2,1)S(1)}, bf16[4,72,10,1]{1,0,3,2:T(4,128)(2,1)S(1)}, u32[]{:S(2)}, u32[]{:S(2)}) collective-permute-start(bf16[4,72,10,1]{1,0,3,2:T(4,128)(2,1)S(1)} %copy.34), channel_id=1, source_target_pairs={{1,0},{2,1},{3,2},{4,3},{5,4},{6,5},{7,6},{0,7},{9,8},{10,9},{11,1... | collective-permute-start | bytes 17288 | tf_op jit(solution)/shard_map/ppermute | solution.py:18
  33.7 4.9 %collective-permute-start.7 = (bf16[4,72,10,1]{1,0,3,2:T(4,128)(2,1)S(1)}, bf16[4,72,10,1]{1,0,3,2:T(4,128)(2,1)S(1)}, u32[]{:S(2)}, u32[]{:S(2)}) collective-permute-start(bf16[4,72,10,1]{1,0,3,2:T(4,128)(2,1)S(1)} %copy.36), channel_id=1, source_target_pairs={{0,1},{1,2},{2,3},{3,4},{4,5},{5,6},{6,7},{7,0},{8,9},{9,10},{10,1... | collective-permute-start | bytes 17288 | tf_op jit(solution)/shard_map/ppermute | solution.py:16
  42.2 4.4 %collective-permute-start.8 = (bf16[4,72,1,128]{3,1,2,0:T(8,128)(2,1)S(1)}, bf16[4,72,1,128]{3,1,2,0:T(8,128)(2,1)S(1)}, u32[]{:S(2)}, u32[]{:S(2)}) collective-permute-start(bf16[4,72,1,128]{3,1,2,0:T(8,128)(2,1)S(1)} %get-tuple-element.14), channel_id=1, source_target_pairs={{8,0},{16,8},{24,16},{0,24},{9,1},{17,9},{25,17},{1,25},{10,2},{18... | collective-permute-start | bytes 221192 | tf_op jit(solution)/shard_map/ppermute | solution.py:18
  43.3 5.3 %collective-permute-start.9 = (bf16[4,72,1,128]{3,1,2,0:T(8,128)(2,1)S(1)}, bf16[4,72,1,128]{3,1,2,0:T(8,128)(2,1)S(1)}, u32[]{:S(2)}, u32[]{:S(2)}) collective-permute-start(bf16[4,72,1,128]{3,1,2,0:T(8,128)(2,1)S(1)} %get-tuple-element.13), channel_id=1, source_target_pairs={{0,8},{8,16},{16,24},{24,0},{1,9},{9,17},{17,25},{25,1},{2,10},{10... | collective-permute-start | bytes 221192 | tf_op jit(solution)/shard_map/ppermute | solution.py:16
  49.3 1.4 %collective-permute-start.10 = (bf16[4,72,10,1]{1,0,3,2:T(4,128)(2,1)S(1)}, bf16[4,72,10,1]{1,0,3,2:T(4,128)(2,1)S(1)}, u32[]{:S(2)}, u32[]{:S(2)}) collective-permute-start(bf16[4,72,10,1]{1,0,3,2:T(4,128)(2,1)S(1)} %copy.38), channel_id=1, source_target_pairs={{1,0},{2,1},{3,2},{4,3},{5,4},{6,5},{7,6},{0,7},{9,8},{10,9},{11,1... | collective-permute-start | bytes 17288 | tf_op jit(solution)/shard_map/ppermute | solution.py:18
  49.7 4.9 %collective-permute-start.11 = (bf16[4,72,10,1]{1,0,3,2:T(4,128)(2,1)S(1)}, bf16[4,72,10,1]{1,0,3,2:T(4,128)(2,1)S(1)}, u32[]{:S(2)}, u32[]{:S(2)}) collective-permute-start(bf16[4,72,10,1]{1,0,3,2:T(4,128)(2,1)S(1)} %copy.40), channel_id=1, source_target_pairs={{0,1},{1,2},{2,3},{3,4},{4,5},{5,6},{6,7},{7,0},{8,9},{9,10},{10,1... | collective-permute-start | bytes 17288 | tf_op jit(solution)/shard_map/ppermute | solution.py:16
  58.8 5.2 %copy-start.2 = (bf16[16,72,72]{2,1,0:T(8,128)(2,1)S(1)}, bf16[16,72,72]{2,1,0:T(8,128)(2,1)}, u32[]{:S(2)}) copy-start(bf16[16,72,72]{2,1,0:T(8,128)(2,1)} %param.11) | copy-start | bytes 497668
  59.8 20.2 %all-to-all-start = ((bf16[4,72,8,128]{3,1,0,2:T(8,128)(2,1)}), bf16[4,72,8,128]{3,1,0,2:T(8,128)(2,1)S(1)}, u32[]{:S(2)}, u32[]{:S(2)}) async-start(bf16[4,72,8,128]{3,1,0,2:T(8,128)(2,1)} %select_bitcast_fusion), calls=%async_computation | async-start | bytes 1179648 | tf_op jit(solution)/shard_map/all_to_all | solution.py:50
where the time goes:
time: 81.9 us; the launch traced here: 81.5 us
  waiting for transfers between devices  39.4 us (48%)
  local copies, waits for them, and re-layouts  16.2 us (20%)
  starting transfers between devices  15.3 us (19%)
  other arithmetic  9.14 us (11%)
  between operations  0.86 us (1%)
    ppermute x6, waiting for transfers between devices, with_halo(): lax.ppermute(tail, axis, [(i, (i + 1) % count) for i in range(count)])  16.9 us
    all_to_all x1, waiting for transfers between devices, per_device(): lax.all_to_all(ordered, 'tile', split_axis=2, concat_axis=2, tiled=True)  15.9 us
    convert_element_type x3, other arithmetic, advect_tile(): return out.astype(jnp.bfloat16)  6.8 us
    ppermute x6, starting transfers between devices, with_halo(): lax.ppermute(head, axis, [((i + 1) % count, i) for i in range(count)])  6.67 us
    ppermute x6, waiting for transfers between devices, with_halo(): lax.ppermute(head, axis, [((i + 1) % count, i) for i in range(count)])  6.61 us
    slice x7, local copies, waits for them, and re-layouts, with_halo(): head = lax.slice_in_dim(cells, 0, width, axis=dim)  5.84 us
    ppermute x6, starting transfers between devices, with_halo(): lax.ppermute(tail, axis, [(i, (i + 1) % count) for i in range(count)])  5.11 us
    all_to_all x1, starting transfers between devices, per_device(): lax.all_to_all(ordered, 'tile', split_axis=2, concat_axis=2, tiled=True)  3.54 us
  transfers between devices with their start and end apart: 13, of which 13 were waited for; matrix products, arithmetic and copies ran while one was open for 6% of the time, Pallas kernels for 0%

commit v1 on v0

--- a/solution.py
+++ b/solution.py
@@ -4,6 +4,16 @@
 from jax.sharding import PartitionSpec as P
 
 STEPS = 3
+
+
+def lead_chunk_up(buf, pos_dim, at_axis):
+    d_next = jnp.concatenate(
+        lax.all_to_all(
+            jnp.stack(jnp.split(buf, lax.axis_size("tile"), axis=pos_dim), axis=0), "tile", 0, 0
+        ),
+        at_axis,
+    )
+    return d_next
 
 
 def with_halo(cells, sides, width):
@@ -47,7 +57,7 @@
     order = jnp.argsort(destination[0])
     band_count = band_table.shape[0]
     ordered = jnp.take(advected, order, axis=2)
-    received = lax.all_to_all(ordered, "tile", split_axis=2, concat_axis=2, tiled=True)
+    received = lead_chunk_up(ordered, 2, 2)
     inverse = diffusion[0]
     diffused = jnp.einsum("kl,tlxy->tkxy", inverse, received, preferred_element_type=jnp.float32)
     diffused16 = diffused.astype(jnp.bfloat16)

time: 81.9 us -> 86.2 us (1.053)
  local copies, waits for them, and re-layouts: 16.2 us -> 21.3 us
    unnamed x13 -> x20, local copies, waits for them, and re-layouts: 1.37 us -> 5.84 us
where the time goes in v1:
time: 86.2 us; the launch traced here: 85.8 us
  waiting for transfers between devices  39.4 us (46%)
  local copies, waits for them, and re-layouts  21.3 us (25%)
  starting transfers between devices  15.3 us (18%)
  other arithmetic  8.33 us (10%)
  between operations  0.87 us (1%)
    ppermute x6, waiting for transfers between devices, with_halo(): lax.ppermute(tail, axis, [(i, (i + 1) % count) for i in range(count)])  16.9 us
    all_to_all x1, waiting for transfers between devices, lead_chunk_up(): lax.all_to_all(jnp.stack(jnp.split(buf, lax.axis_size('tile'), axis=pos_d...  15.9 us
    convert_element_type x3, other arithmetic, advect_tile(): return out.astype(jnp.bfloat16)  6.8 us
    ppermute x6, starting transfers between devices, with_halo(): lax.ppermute(head, axis, [((i + 1) % count, i) for i in range(count)])  6.67 us
    ppermute x6, waiting for transfers between devices, with_halo(): lax.ppermute(head, axis, [((i + 1) % count, i) for i in range(count)])  6.6 us
    slice x7, local copies, waits for them, and re-layouts, with_halo(): head = lax.slice_in_dim(cells, 0, width, axis=dim)  5.84 us
    unnamed x20, local copies, waits for them, and re-layouts  5.84 us
    ppermute x6, starting transfers between devices, with_halo(): lax.ppermute(tail, axis, [(i, (i + 1) % count) for i in range(count)])  5.11 us
  transfers between devices with their start and end apart: 13, of which 13 were waited for; matrix products, arithmetic and copies ran while one was open for 6% of the time, Pallas kernels for 0%

profile of v1, /device:TPU:0, one launch (start us, length us, event | category | flops | bytes accessed | tf_op | source)
XLA Modules:
  0.0 85.8 jit_solution(786491054482240294)
XLA Ops:
  0.0 1.2 %copy.33 = bf16[4,72,8,128]{3,1,2,0:T(8,128)(2,1)S(1)} copy(bf16[4,72,8,128]{3,2,1,0:T(8,128)(2,1)} %param.6) | data formatting | bytes 1179648 | tf_op args[0]
  1.2 3.0 %collective-permute-start.1 = (bf16[4,72,1,128]{3,1,2,0:T(8,128)(2,1)S(1)}, bf16[4,72,1,128]{3,1,2,0:T(8,128)(2,1)S(1)}, u32[]{:S(2)}, u32[]{:S(2)}) collective-permute-start(bf16[4,72,1,128]{3,1,2,0:T(8,128)(2,1)S(1)} %get-tuple-element.18), channel_id=1, source_target_pairs={{0,8},{8,16},{16,24},{24,0},{1,9},{9,17},{17,25},{25,1},{2,10},{10... | collective-permute-start | bytes 221192 | tf_op jit(solution)/shard_map/ppermute | solution.py:26
  4.2 1.0 %collective-permute-start = (bf16[4,72,1,128]{3,1,2,0:T(8,128)(2,1)S(1)}, bf16[4,72,1,128]{3,1,2,0:T(8,128)(2,1)S(1)}, u32[]{:S(2)}, u32[]{:S(2)}) collective-permute-start(bf16[4,72,1,128]{3,1,2,0:T(8,128)(2,1)S(1)} %get-tuple-element.17), channel_id=1, source_target_pairs={{8,0},{16,8},{24,16},{0,24},{9,1},{17,9},{25,17},{1,25},{10,2},{18... | collective-permute-start | bytes 221192 | tf_op jit(solution)/shard_map/ppermute | solution.py:28
  5.3 2.5 %collective-permute-done.1 = bf16[4,72,1,128]{3,1,2,0:T(8,128)(2,1)S(1)} collective-permute-done((bf16[4,72,1,128]{3,1,2,0:T(8,128)(2,1)S(1)}, bf16[4,72,1,128]{3,1,2,0:T(8,128)(2,1)S(1)}, u32[]{:S(2)}, u32[]{:S(2)}) %collective-permute-start.1) | collective-permute-done | bytes 73760 | tf_op jit(solution)/shard_map/ppermute | solution.py:26
  7.9 1.4 %collective-permute-done = bf16[4,72,1,128]{3,1,2,0:T(8,128)(2,1)S(1)} collective-permute-done((bf16[4,72,1,128]{3,1,2,0:T(8,128)(2,1)S(1)}, bf16[4,72,1,128]{3,1,2,0:T(8,128)(2,1)S(1)}, u32[]{:S(2)}, u32[]{:S(2)}) %collective-permute-start) | collective-permute-done | bytes 73760 | tf_op jit(solution)/shard_map/ppermute | solution.py:28
  9.3 1.1 %fusion.45 = (bf16[4,72,10,1]{3,1,2,0:T(8,128)(2,1)}, bf16[4,72,10,1]{3,1,2,0:T(8,128)(2,1)S(1)}) fusion(bf16[4,72,10,128]{3,1,2,0:T(8,128)(2,1)S(1)} %constant_dynamic-update-slice_fusion), kind=kLoop, calls=%fused_computation.114 | loop fusion | bytes 23040 | tf_op jit(solution)/shard_map/slice | solution.py:22
  10.4 1.5 %copy.42 = bf16[4,72,10,1]{1,0,3,2:T(4,128)(2,1)S(1)} copy(bf16[4,72,10,1]{3,1,2,0:T(8,128)(2,1)} %get-tuple-element.11) | data formatting | bytes 11520 | tf_op jit(solution)/shard_map/slice | solution.py:22
  11.9 2.2 %collective-permute-start.2 = (bf16[4,72,10,1]{1,0,3,2:T(4,128)(2,1)S(1)}, bf16[4,72,10,1]{1,0,3,2:T(4,128)(2,1)S(1)}, u32[]{:S(2)}, u32[]{:S(2)}) collective-permute-start(bf16[4,72,10,1]{1,0,3,2:T(4,128)(2,1)S(1)} %copy.42), channel_id=1, source_target_pairs={{1,0},{2,1},{3,2},{4,3},{5,4},{6,5},{7,6},{0,7},{9,8},{10,9},{11,1... | collective-permute-start | bytes 17288 | tf_op jit(solution)/shard_map/ppermute | solution.py:28
  15.5 1.2 %copy.43 = bf16[4,72,10,1]{3,1,2,0:T(8,128)(2,1)} copy(bf16[4,72,10,1]{1,0,3,2:T(4,128)(2,1)S(1)} %collective-permute-done.2) | data formatting | bytes 11520 | tf_op jit(solution)/shard_map/ppermute | solution.py:28
  16.8 2.6 %collective-permute-done.3 = bf16[4,72,10,1]{1,0,3,2:T(4,128)(2,1)S(1)} collective-permute-done((bf16[4,72,10,1]{1,0,3,2:T(4,128)(2,1)S(1)}, bf16[4,72,10,1]{1,0,3,2:T(4,128)(2,1)S(1)}, u32[]{:S(2)}, u32[]{:S(2)}) %collective-permute-start.3) | collective-permute-done | bytes 5792 | tf_op jit(solution)/shard_map/ppermute | solution.py:26
  19.4 1.2 %copy.45 = bf16[4,72,10,1]{3,1,2,0:T(8,128)(2,1)} copy(bf16[4,72,10,1]{1,0,3,2:T(4,128)(2,1)S(1)} %collective-permute-done.3) | data formatting | bytes 11520 | tf_op jit(solution)/shard_map/ppermute | solution.py:26
  20.6 2.5 %fusion.5 = bf16[4,72,8,128]{3,1,2,0:T(8,128)(2,1)S(1)} fusion(bf16[4,72,8,128]{3,1,2,0:T(8,128)(2,1)S(1)} %copy.33, bf16[4,72,10,128]{3,1,2,0:T(8,128)(2,1)S(1)} %constant_dynamic-update-slice_fusion, bf16[4,72,10,1]{3,1,2,0:T(8,128)(2,1)} %copy.45, bf16[4,72,10,1]{3,1,2,0:T(8,128)(2,1)} %copy.43, bf16[4,72,1,128]{3,1,2,0:T(8,128)(2,1)S(1)} %collective-permute-done.1, ...), kind=kLoop, calls=%fused_computation.31 | loop fusion | flops 9732096 | bytes 3255552 | tf_op jit(solution)/shard_map/convert_element_type | solution.py:45
  23.1 2.2 %collective-permute-start.4 = (bf16[4,72,1,128]{3,1,2,0:T(8,128)(2,1)S(1)}, bf16[4,72,1,128]{3,1,2,0:T(8,128)(2,1)S(1)}, u32[]{:S(2)}, u32[]{:S(2)}) collective-permute-start(bf16[4,72,1,128]{3,1,2,0:T(8,128)(2,1)S(1)} %get-tuple-element.16), channel_id=1, source_target_pairs={{8,0},{16,8},{24,16},{0,24},{9,1},{17,9},{25,17},{1,25},{10,2},{18... | collective-permute-start | bytes 221192 | tf_op jit(solution)/shard_map/ppermute | solution.py:28
  25.5 1.0 %sort.17 = (s32[8]{0:T(128)}, s32[8]{0:T(128)S(1)}) sort(s32[8]{0:T(128)S(1)} %bitcast.67, s32[8]{0:T(128)S(1)} %iota.9), dimensions={0}, to_apply=%region_0.0 | sort | flops 24 | bytes 128 | tf_op jit(solution)/shard_map/jit(argsort)/sort | solution.py:57
  26.4 1.3 %collective-permute-done.4 = bf16[4,72,1,128]{3,1,2,0:T(8,128)(2,1)S(1)} collective-permute-done((bf16[4,72,1,128]{3,1,2,0:T(8,128)(2,1)S(1)}, bf16[4,72,1,128]{3,1,2,0:T(8,128)(2,1)S(1)}, u32[]{:S(2)}, u32[]{:S(2)}) %collective-permute-start.4) | collective-permute-done | bytes 73760 | tf_op jit(solution)/shard_map/ppermute | solution.py:28
  27.7 2.9 %collective-permute-done.5 = bf16[4,72,1,128]{3,1,2,0:T(8,128)(2,1)S(1)} collective-permute-done((bf16[4,72,1,128]{3,1,2,0:T(8,128)(2,1)S(1)}, bf16[4,72,1,128]{3,1,2,0:T(8,128)(2,1)S(1)}, u32[]{:S(2)}, u32[]{:S(2)}) %collective-permute-start.5) | collective-permute-done | bytes 73760 | tf_op jit(solution)/shard_map/ppermute | solution.py:26
  30.7 1.1 %fusion.44 = (bf16[4,72,10,1]{3,1,2,0:T(8,128)(2,1)}, bf16[4,72,10,1]{3,1,2,0:T(8,128)(2,1)S(1)}) fusion(bf16[4,72,10,128]{3,1,2,0:T(8,128)(2,1)S(1)} %pad_maximum_fusion), kind=kLoop, calls=%fused_computation.113 | loop fusion | bytes 23040 | tf_op jit(solution)/shard_map/slice | solution.py:22
  31.8 1.4 %copy.47 = bf16[4,72,10,1]{1,0,3,2:T(4,128)(2,1)S(1)} copy(bf16[4,72,10,1]{3,1,2,0:T(8,128)(2,1)} %get-tuple-element.9) | data formatting | bytes 11520 | tf_op jit(solution)/shard_map/slice | solution.py:22
  35.2 3.5 %collective-permute-done.7 = bf16[4,72,10,1]{1,0,3,2:T(4,128)(2,1)S(1)} collective-permute-done((bf16[4,72,10,1]{1,0,3,2:T(4,128)(2,1)S(1)}, bf16[4,72,10,1]{1,0,3,2:T(4,128)(2,1)S(1)}, u32[]{:S(2)}, u32[]{:S(2)}) %collective-permute-start.7) | collective-permute-done | bytes 5792 | tf_op jit(solution)/shard_map/ppermute | solution.py:26
  38.6 1.2 %copy.50 = bf16[4,72,10,1]{3,1,2,0:T(8,128)(2,1)} copy(bf16[4,72,10,1]{1,0,3,2:T(4,128)(2,1)S(1)} %collective-permute-done.7) | data formatting | bytes 11520 | tf_op jit(solution)/shard_map/ppermute | solution.py:26
  39.8 2.3 %fusion.13 = bf16[4,72,8,128]{3,1,2,0:T(8,128)(2,1)S(1)} fusion(bf16[4,72,8,128]{3,1,2,0:T(8,128)(2,1)S(1)} %fusion.5, bf16[4,72,10,1]{3,1,2,0:T(8,128)(2,1)} %copy.50, bf16[4,72,1,128]{3,1,2,0:T(8,128)(2,1)S(1)} %collective-permute-done.4, bf16[4,72,1,128]{3,1,2,0:T(8,128)(2,1)S(1)} %collective-permute-done.5, bf16[4,72,10,1]{3,1,2,0:T(8,128)(2,1)S(1)} %copy.48, ...), kind=kLoop, calls=%fused_computation.39 | loop fusion | flops 12091392 | bytes 2518272 | tf_op jit(solution)/shard_map/convert_element_type | solution.py:45
  42.2 1.2 %collective-permute-start.8 = (bf16[4,72,1,128]{3,1,2,0:T(8,128)(2,1)S(1)}, bf16[4,72,1,128]{3,1,2,0:T(8,128)(2,1)S(1)}, u32[]{:S(2)}, u32[]{:S(2)}) collective-permute-start(bf16[4,72,1,128]{3,1,2,0:T(8,128)(2,1)S(1)} %get-tuple-element.14), channel_id=1, source_target_pairs={{8,0},{16,8},{24,16},{0,24},{9,1},{17,9},{25,17},{1,25},{10,2},{18... | collective-permute-start | bytes 221192 | tf_op jit(solution)/shard_map/ppermute | solution.py:28
  43.3 0.9 %collective-permute-start.9 = (bf16[4,72,1,128]{3,1,2,0:T(8,128)(2,1)S(1)}, bf16[4,72,1,128]{3,1,2,0:T(8,128)(2,1)S(1)}, u32[]{:S(2)}, u32[]{:S(2)}) collective-permute-start(bf16[4,72,1,128]{3,1,2,0:T(8,128)(2,1)S(1)} %get-tuple-element.13), channel_id=1, source_target_pairs={{0,8},{8,16},{16,24},{24,0},{1,9},{9,17},{17,25},{25,1},{2,10},{10... | collective-permute-start | bytes 221192 | tf_op jit(solution)/shard_map/ppermute | solution.py:26
  44.2 2.3 %collective-permute-done.8 = bf16[4,72,1,128]{3,1,2,0:T(8,128)(2,1)S(1)} collective-permute-done((bf16[4,72,1,128]{3,1,2,0:T(8,128)(2,1)S(1)}, bf16[4,72,1,128]{3,1,2,0:T(8,128)(2,1)S(1)}, u32[]{:S(2)}, u32[]{:S(2)}) %collective-permute-start.8) | collective-permute-done | bytes 73760 | tf_op jit(solution)/shard_map/ppermute | solution.py:28
  46.6 2.0 %collective-permute-done.9 = bf16[4,72,1,128]{3,1,2,0:T(8,128)(2,1)S(1)} collective-permute-done((bf16[4,72,1,128]{3,1,2,0:T(8,128)(2,1)S(1)}, bf16[4,72,1,128]{3,1,2,0:T(8,128)(2,1)S(1)}, u32[]{:S(2)}, u32[]{:S(2)}) %collective-permute-start.9) | collective-permute-done | bytes 73760 | tf_op jit(solution)/shard_map/ppermute | solution.py:26
  51.2 3.5 %collective-permute-done.11 = bf16[4,72,10,1]{1,0,3,2:T(4,128)(2,1)S(1)} collective-permute-done((bf16[4,72,10,1]{1,0,3,2:T(4,128)(2,1)S(1)}, bf16[4,72,10,1]{1,0,3,2:T(4,128)(2,1)S(1)}, u32[]{:S(2)}, u32[]{:S(2)}) %collective-permute-start.11) | collective-permute-done | bytes 5792 | tf_op jit(solution)/shard_map/ppermute | solution.py:26
  55.1 2.0 %fusion.21 = bf16[4,72,8,128]{3,1,2,0:T(8,128)(2,1)} fusion(bf16[4,72,8,128]{3,1,2,0:T(8,128)(2,1)S(1)} %fusion.13, bf16[4,72,10,1]{3,1,2,0:T(8,128)(2,1)S(1)} %copy.54, bf16[4,72,1,128]{3,1,2,0:T(8,128)(2,1)S(1)} %collective-permute-done.8, bf16[4,72,1,128]{3,1,2,0:T(8,128)(2,1)S(1)} %collective-permute-done.9, bf16[4,72,10,1]{3,1,2,0:T(8,128)(2,1)S(1)} %copy.52, ...), kind=kLoop, calls=%fused_computation.47 | loop fusion | flops 12091392 | bytes 2518272 | tf_op jit(solution)/shard_map/convert_element_type | solution.py:45
  57.1 1.7 %gather_fusion = bf16[8,4,72,128]{3,2,1,0:T(8,128)(2,1)S(1)} fusion(bf16[4,72,8,128]{3,1,2,0:T(8,128)(2,1)} %fusion.21, s32[1024]{0:T(1024)S(1)} %pad_clamp_fusion), kind=kCustom, calls=%fused_computation | custom fusion | bytes 1179680 | tf_op jit(solution)/shard_map/jit(_take)/gather | solution.py:59
  59.0 0.6 fusion.40
  64.1 3.5 %all-to-all-start = ((bf16[8,4,72,1,128]{4,2,1,3,0:T(8,128)(2,1)}), bf16[8,4,72,1,128]{4,2,1,3,0:T(8,128)(2,1)S(1)}, u32[]{:S(2)}, u32[]{:S(2)}) async-start(bf16[8,4,72,1,128]{4,2,1,3,0:T(8,128)(2,1)} %fusion.33), calls=%async_computation | async-start | bytes 1179648 | tf_op jit(solution)/shard_map/all_to_all | solution.py:11
  68.5 15.9 %all-to-all-done = bf16[8,4,72,1,128]{4,2,1,3,0:T(8,128)(2,1)S(1)} async-done(((bf16[8,4,72,1,128]{4,2,1,3,0:T(8,128)(2,1)}), bf16[8,4,72,1,128]{4,2,1,3,0:T(8,128)(2,1)S(1)}, u32[]{:S(2)}, u32[]{:S(2)}) %all-to-all-start) | async-done | bytes 589856 | tf_op jit(solution)/shard_map/all_to_all | solution.py:11
  84.9 0.9 %copy.56 = bf16[4,72,8,128]{3,2,1,0:T(8,128)(2,1)} copy(bf16[4,72,8,128]{3,1,2,0:T(8,128)(2,1)S(1)} %fusion.1) | data formatting | bytes 1179648 | tf_op jit(solution)/shard_map/convert_element_type | solution.py:67
  (56 shorter events, 12.0 us)
Async XLA Ops:
  0.0 84.3 %copy-start = (bf16[1,72,72]{2,1,0:T(8,128)(2,1)S(1)}, bf16[1,72,72]{2,1,0:T(8,128)(2,1)}, u32[]{:S(2)}) copy-start(bf16[1,72,72]{2,1,0:T(8,128)(2,1)} %param.9) | copy-start | bytes 31108
  0.0 7.8 %copy-start.1 = (bf16[4,72,8,128]{3,2,1,0:T(8,128)(2,1)S(1)}, bf16[4,72,8,128]{3,2,1,0:T(8,128)(2,1)}, u32[]{:S(2)}) copy-start(bf16[4,72,8,128]{3,2,1,0:T(8,128)(2,1)} %param.6) | copy-start | bytes 1769476
  1.2 6.5 %collective-permute-start.1 = (bf16[4,72,1,128]{3,1,2,0:T(8,128)(2,1)S(1)}, bf16[4,72,1,128]{3,1,2,0:T(8,128)(2,1)S(1)}, u32[]{:S(2)}, u32[]{:S(2)}) collective-permute-start(bf16[4,72,1,128]{3,1,2,0:T(8,128)(2,1)S(1)} %get-tuple-element.18), channel_id=1, source_target_pairs={{0,8},{8,16},{16,24},{24,0},{1,9},{9,17},{17,25},{25,1},{2,10},{10... | collective-permute-start | bytes 221192 | tf_op jit(solution)/shard_map/ppermute | solution.py:26
  4.2 5.1 %collective-permute-start = (bf16[4,72,1,128]{3,1,2,0:T(8,128)(2,1)S(1)}, bf16[4,72,1,128]{3,1,2,0:T(8,128)(2,1)S(1)}, u32[]{:S(2)}, u32[]{:S(2)}) collective-permute-start(bf16[4,72,1,128]{3,1,2,0:T(8,128)(2,1)S(1)} %get-tuple-element.17), channel_id=1, source_target_pairs={{8,0},{16,8},{24,16},{0,24},{9,1},{17,9},{25,17},{1,25},{10,2},{18... | collective-permute-start | bytes 221192 | tf_op jit(solution)/shard_map/ppermute | solution.py:28
  10.4 4.1 %copy-start.3 = (bf16[2,72,8,128]{3,2,1,0:T(8,128)(2,1)S(1)}, bf16[2,72,8,128]{3,2,1,0:T(8,128)(2,1)}, u32[]{:S(2)}) copy-start(bf16[2,72,8,128]{3,2,1,0:T(8,128)(2,1)} %param.7) | copy-start | bytes 884740
  11.9 3.6 %collective-permute-start.2 = (bf16[4,72,10,1]{1,0,3,2:T(4,128)(2,1)S(1)}, bf16[4,72,10,1]{1,0,3,2:T(4,128)(2,1)S(1)}, u32[]{:S(2)}, u32[]{:S(2)}) collective-permute-start(bf16[4,72,10,1]{1,0,3,2:T(4,128)(2,1)S(1)} %copy.42), channel_id=1, source_target_pairs={{1,0},{2,1},{3,2},{4,3},{5,4},{6,5},{7,6},{0,7},{9,8},{10,9},{11,1... | collective-permute-start | bytes 17288 | tf_op jit(solution)/shard_map/ppermute | solution.py:28
  14.5 4.9 %collective-permute-start.3 = (bf16[4,72,10,1]{1,0,3,2:T(4,128)(2,1)S(1)}, bf16[4,72,10,1]{1,0,3,2:T(4,128)(2,1)S(1)}, u32[]{:S(2)}, u32[]{:S(2)}) collective-permute-start(bf16[4,72,10,1]{1,0,3,2:T(4,128)(2,1)S(1)} %copy.44), channel_id=1, source_target_pairs={{0,1},{1,2},{2,3},{3,4},{4,5},{5,6},{6,7},{7,0},{8,9},{9,10},{10,1... | collective-permute-start | bytes 17288 | tf_op jit(solution)/shard_map/ppermute | solution.py:26
  20.6 4.8 %copy-start.4 = (s32[1,8]{1,0:T(1,128)S(1)}, s32[1,8]{1,0:T(1,128)}, u32[]{:S(2)}) copy-start(s32[1,8]{1,0:T(1,128)} %param.8) | copy-start | bytes 100
  23.1 4.6 %collective-permute-start.4 = (bf16[4,72,1,128]{3,1,2,0:T(8,128)(2,1)S(1)}, bf16[4,72,1,128]{3,1,2,0:T(8,128)(2,1)S(1)}, u32[]{:S(2)}, u32[]{:S(2)}) collective-permute-start(bf16[4,72,1,128]{3,1,2,0:T(8,128)(2,1)S(1)} %get-tuple-element.16), channel_id=1, source_target_pairs={{8,0},{16,8},{24,16},{0,24},{9,1},{17,9},{25,17},{1,25},{10,2},{18... | collective-permute-start | bytes 221192 | tf_op jit(solution)/shard_map/ppermute | solution.py:28
  25.4 5.3 %collective-permute-start.5 = (bf16[4,72,1,128]{3,1,2,0:T(8,128)(2,1)S(1)}, bf16[4,72,1,128]{3,1,2,0:T(8,128)(2,1)S(1)}, u32[]{:S(2)}, u32[]{:S(2)}) collective-permute-start(bf16[4,72,1,128]{3,1,2,0:T(8,128)(2,1)S(1)} %get-tuple-element.15), channel_id=1, source_target_pairs={{0,8},{8,16},{16,24},{24,0},{1,9},{9,17},{17,25},{25,1},{2,10},{10... | collective-permute-start | bytes 221192 | tf_op jit(solution)/shard_map/ppermute | solution.py:26
  33.3 1.4 %collective-permute-start.6 = (bf16[4,72,10,1]{1,0,3,2:T(4,128)(2,1)S(1)}, bf16[4,72,10,1]{1,0,3,2:T(4,128)(2,1)S(1)}, u32[]{:S(2)}, u32[]{:S(2)}) collective-permute-start(bf16[4,72,10,1]{1,0,3,2:T(4,128)(2,1)S(1)} %copy.47), channel_id=1, source_target_pairs={{1,0},{2,1},{3,2},{4,3},{5,4},{6,5},{7,6},{0,7},{9,8},{10,9},{11,1... | collective-permute-start | bytes 17288 | tf_op jit(solution)/shard_map/ppermute | solution.py:28
  33.7 4.9 %collective-permute-start.7 = (bf16[4,72,10,1]{1,0,3,2:T(4,128)(2,1)S(1)}, bf16[4,72,10,1]{1,0,3,2:T(4,128)(2,1)S(1)}, u32[]{:S(2)}, u32[]{:S(2)}) collective-permute-start(bf16[4,72,10,1]{1,0,3,2:T(4,128)(2,1)S(1)} %copy.49), channel_id=1, source_target_pairs={{0,1},{1,2},{2,3},{3,4},{4,5},{5,6},{6,7},{7,0},{8,9},{9,10},{10,1... | collective-permute-start | bytes 17288 | tf_op jit(solution)/shard_map/ppermute | solution.py:26
  42.2 4.4 %collective-permute-start.8 = (bf16[4,72,1,128]{3,1,2,0:T(8,128)(2,1)S(1)}, bf16[4,72,1,128]{3,1,2,0:T(8,128)(2,1)S(1)}, u32[]{:S(2)}, u32[]{:S(2)}) collective-permute-start(bf16[4,72,1,128]{3,1,2,0:T(8,128)(2,1)S(1)} %get-tuple-element.14), channel_id=1, source_target_pairs={{8,0},{16,8},{24,16},{0,24},{9,1},{17,9},{25,17},{1,25},{10,2},{18... | collective-permute-start | bytes 221192 | tf_op jit(solution)/shard_map/ppermute | solution.py:28
  43.3 5.3 %collective-permute-start.9 = (bf16[4,72,1,128]{3,1,2,0:T(8,128)(2,1)S(1)}, bf16[4,72,1,128]{3,1,2,0:T(8,128)(2,1)S(1)}, u32[]{:S(2)}, u32[]{:S(2)}) collective-permute-start(bf16[4,72,1,128]{3,1,2,0:T(8,128)(2,1)S(1)} %get-tuple-element.13), channel_id=1, source_target_pairs={{0,8},{8,16},{16,24},{24,0},{1,9},{9,17},{17,25},{25,1},{2,10},{10... | collective-permute-start | bytes 221192 | tf_op jit(solution)/shard_map/ppermute | solution.py:26
  49.3 1.4 %collective-permute-start.10 = (bf16[4,72,10,1]{1,0,3,2:T(4,128)(2,1)S(1)}, bf16[4,72,10,1]{1,0,3,2:T(4,128)(2,1)S(1)}, u32[]{:S(2)}, u32[]{:S(2)}) collective-permute-start(bf16[4,72,10,1]{1,0,3,2:T(4,128)(2,1)S(1)} %copy.51), channel_id=1, source_target_pairs={{1,0},{2,1},{3,2},{4,3},{5,4},{6,5},{7,6},{0,7},{9,8},{10,9},{11,1... | collective-permute-start | bytes 17288 | tf_op jit(solution)/shard_map/ppermute | solution.py:28
  49.7 4.9 %collective-permute-start.11 = (bf16[4,72,10,1]{1,0,3,2:T(4,128)(2,1)S(1)}, bf16[4,72,10,1]{1,0,3,2:T(4,128)(2,1)S(1)}, u32[]{:S(2)}, u32[]{:S(2)}) collective-permute-start(bf16[4,72,10,1]{1,0,3,2:T(4,128)(2,1)S(1)} %copy.53), channel_id=1, source_target_pairs={{0,1},{1,2},{2,3},{3,4},{4,5},{5,6},{6,7},{7,0},{8,9},{9,10},{10,1... | collective-permute-start | bytes 17288 | tf_op jit(solution)/shard_map/ppermute | solution.py:26
  59.0 9.3 %copy-start.2 = (bf16[16,72,72]{2,1,0:T(8,128)(2,1)S(1)}, bf16[16,72,72]{2,1,0:T(8,128)(2,1)}, u32[]{:S(2)}) copy-start(bf16[16,72,72]{2,1,0:T(8,128)(2,1)} %param.11) | copy-start | bytes 497668
  64.1 20.2 %all-to-all-start = ((bf16[8,4,72,1,128]{4,2,1,3,0:T(8,128)(2,1)}), bf16[8,4,72,1,128]{4,2,1,3,0:T(8,128)(2,1)S(1)}, u32[]{:S(2)}, u32[]{:S(2)}) async-start(bf16[8,4,72,1,128]{4,2,1,3,0:T(8,128)(2,1)} %fusion.33), calls=%async_computation | async-start | bytes 1179648 | tf_op jit(solution)/shard_map/all_to_all | solution.py:11
